TPU v7x, 512 devices: a whole 4x8x8 slice. The times are simulated.
512 devices in a mesh: dp: 8 (over y), expert: 64 (over x, z, core).
Axes of the slice: x: 4, y: 8, z: 8, core: 2. Of those that a mesh axis runs over, the one named last changes fastest.
Arguments:
- tokens: bfloat16 [65536, 3584], P(('dp', 'expert')), may hold values from -6 to 6
- out_cotangent: bfloat16 [65536, 3584], P(('dp', 'expert')), may hold values from -6 to 6
- expert_ids: int32 [65536, 8], P(('dp', 'expert')), may hold values from 0 to 255, as said below
- gate_fixed: int32 [65536, 8], P(('dp', 'expert')), may hold values from 4096 to 65535
- w_gate: bfloat16 [64, 3584, 128], P('expert', 'dp'), may hold values from -0.09375 to 0.09375
- w_up: bfloat16 [64, 3584, 128], P('expert', 'dp'), may hold values from -0.09375 to 0.09375
- w_down: bfloat16 [64, 3584, 128], P('expert', 'dp'), may hold values from -0.125 to 0.125
Outputs:
- layer_out: bfloat16 [65536, 3584], P(('dp', 'expert'))
- token_grad: bfloat16 [65536, 3584], P(('dp', 'expert'))
- grad_gate: float32 [64, 3584, 128], P('expert', 'dp')
- grad_up: float32 [64, 3584, 128], P('expert', 'dp')
- grad_down: float32 [64, 3584, 128], P('expert', 'dp')
Inputs may be any that keep to these rules, and one draw needn't show every extreme that they name: `expert_ids`: each row names 8 different experts. Within the 128 rows of one device each expert below 4 is named by 1 to 4 rows; in every draw one expert below 4 is named by exactly 4 rows on every device.
All inputs are finite; a program needn't handle non-finite values.
Results may differ from a plain program's by a relative error of at most 0.014.
Values may be sent and summed in bfloat16 or wider, within the bound.
No kernel may reach another device: no remote copies, remote signals or barrier semaphores. Data moves between devices by JAX's collectives and lax.ppermute only.
A program may use at most 128 MiB of HBM per device.

v0:
```python
import jax
import jax.numpy as jnp
from jax import lax
from jax.sharding import PartitionSpec as P

SPLIT = 16
CAP = 4
SCALE = 2.0 ** (-16)
HIGH = lax.Precision.HIGHEST


def routing(ids, gates, window, capacity):
    wanted = jnp.arange(window, dtype=jnp.int32)
    hits = ids[:, :, None] == wanted[None, None, :]
    member = jnp.any(hits, axis=1)
    weight = jnp.sum(jnp.where(hits, gates[:, :, None], 0), axis=1).astype(jnp.float32) * SCALE
    rank = jnp.cumsum(member.astype(jnp.int32), axis=0) - 1
    slots = jnp.arange(capacity, dtype=jnp.int32)
    pick = jnp.logical_and(member[:, :, None], rank[:, :, None] == slots[None, None, :])
    select = jnp.where(pick, 1.0, 0.0).astype(jnp.float32)
    slot_gate = jnp.sum(select * weight[:, :, None], axis=0)
    return (select, slot_gate)


def expert_math(inputs, cotangents, gate_w, up_w, down_w):
    gate_pre = jnp.einsum("prf,pfh->rh", inputs, gate_w, preferred_element_type=jnp.float32)
    up_pre = jnp.einsum("prf,pfh->rh", inputs, up_w, preferred_element_type=jnp.float32)
    sig = jax.nn.sigmoid(gate_pre)
    act = gate_pre * sig
    hidden = (act * up_pre).astype(jnp.bfloat16)
    partial_out = jnp.einsum("rh,pfh->prf", hidden, down_w, preferred_element_type=jnp.float32)
    d_hidden = jnp.einsum("prf,pfh->rh", cotangents, down_w, preferred_element_type=jnp.float32)
    d_gate = (d_hidden * up_pre * sig * (1.0 + gate_pre * (1.0 - sig))).astype(jnp.bfloat16)
    d_up = (d_hidden * act).astype(jnp.bfloat16)
    partial_grad = jnp.einsum(
        "rh,pfh->prf", d_gate, gate_w, preferred_element_type=jnp.float32
    ) + jnp.einsum("rh,pfh->prf", d_up, up_w, preferred_element_type=jnp.float32)
    term = jnp.concatenate(
        [
            jnp.einsum("prf,rh->pfh", inputs, d_gate, preferred_element_type=jnp.float32),
            jnp.einsum("prf,rh->pfh", inputs, d_up, preferred_element_type=jnp.float32),
            jnp.einsum("prf,rh->pfh", cotangents, hidden, preferred_element_type=jnp.float32),
        ],
        axis=2,
    )
    return (partial_out, partial_grad, term.reshape(-1, term.shape[2]))


def per_device(tokens, out_cotangent, expert_ids, gate_fixed, w_gate, w_up, w_down):
    tok_rows, width = tokens.shape
    groups = lax.axis_size("expert")
    window = groups // SPLIT
    hid = w_gate.shape[2]
    parts = 1
    feat = width // parts
    select, slot_gate = routing(expert_ids, gate_fixed, window, CAP)
    select_b = select.astype(jnp.bfloat16)
    tok3 = tokens.reshape(tok_rows, parts, feat)
    cot3 = out_cotangent.reshape(tok_rows, parts, feat)
    slot_tokens = jnp.einsum(
        "tec,tsf->escf", select_b, tok3, preferred_element_type=jnp.float32
    ).astype(jnp.bfloat16)
    picked = jnp.einsum("tec,tsf->escf", select_b, cot3, preferred_element_type=jnp.float32)
    slot_cot = (picked * slot_gate[:, None, :, None]).astype(jnp.bfloat16)
    payload = jnp.stack([slot_tokens, slot_cot], axis=2)
    gate_full, up_full, down_full = (
        lax.all_gather(w_gate, "dp", axis=1, tiled=True),
        lax.all_gather(w_up, "dp", axis=1, tiled=True),
        lax.all_gather(w_down, "dp", axis=1, tiled=True),
    )
    outgoing = jnp.broadcast_to(payload, (window, SPLIT, 2, CAP, width)).reshape(
        groups, 2, CAP, width
    )
    arrived = lax.all_to_all(outgoing, "expert", split_axis=0, concat_axis=0, tiled=True)
    pieces = arrived[None]
    inputs = pieces[:, :, 0].reshape(parts, groups * CAP, feat)
    cotangents = pieces[:, :, 1].reshape(parts, groups * CAP, feat)
    partial_out, partial_grad, term = expert_math(inputs, cotangents, gate_full, up_full, down_full)
    summed = lax.psum_scatter(
        term.astype(jnp.bfloat16), "dp", scatter_dimension=0, tiled=True
    ).astype(jnp.float32)
    grad_gate = summed[:, :hid][None]
    grad_up = summed[:, hid : 2 * hid][None]
    grad_down = summed[:, 2 * hid :][None]
    results = jnp.stack(
        [
            partial_out.reshape(parts, groups, CAP, feat),
            partial_grad.reshape(parts, groups, CAP, feat),
        ],
        axis=2,
    )
    returned = lax.all_to_all(
        results[0].astype(jnp.bfloat16), "expert", split_axis=0, concat_axis=0, tiled=True
    ).astype(jnp.float32)
    combined = jnp.sum(
        returned.reshape(window, SPLIT, 2, CAP, width), axis=1, keepdims=True
    ).astype(jnp.bfloat16)
    weighted = select * slot_gate[None, :, :]
    layer_out = jnp.einsum(
        "tec,ehcf->thf", weighted, combined[:, :, 0].astype(jnp.float32), precision=HIGH
    )
    token_grad = jnp.einsum(
        "tec,ehcf->thf", select, combined[:, :, 1].astype(jnp.float32), precision=HIGH
    )
    return (
        layer_out.reshape(tok_rows, width).astype(jnp.bfloat16),
        token_grad.reshape(tok_rows, width).astype(jnp.bfloat16),
        grad_gate,
        grad_up,
        grad_down,
    )


def solution(mesh):
    return jax.shard_map(
        per_device,
        mesh=mesh,
        in_specs=(
            P(("dp", "expert"), None),
            P(("dp", "expert"), None),
            P(("dp", "expert"), None),
            P(("dp", "expert"), None),
            P("expert", "dp", None),
            P("expert", "dp", None),
            P("expert", "dp", None),
        ),
        out_specs=(
            P(("dp", "expert"), None),
            P(("dp", "expert"), None),
            P("expert", "dp", None),
            P("expert", "dp", None),
            P("expert", "dp", None),
        ),
        check_vma=False,
    )
```

profile of v0, /device:TPU:1, one launch (start us, length us, event | category | flops | bytes accessed | tf_op | source)
XLA Modules:
  0.0 262.6 jit_solution(5232182075128742454)
XLA Ops:
  7.2 0.8 fusion.25
  8.3 0.7 select_reduce_fusion
  9.5 1.4 fusion.11
  11.2 2.9 %broadcast_in_dim.54 = bf16[4,16,2,4,3584]{4,3,2,1,0:T(4,128)(2,1)} broadcast(bf16[4,2,4,3584]{3,2,1,0:T(4,128)(2,1)S(1)} %copy.43), dimensions={0,2,3,4} | broadcast | bytes 3899392 | tf_op jit(solution)/shard_map/broadcast_in_dim | solution.py:71
  14.1 15.1 %all-to-all-start = ((bf16[64,2,4,3584]{3,2,1,0:T(4,128)(2,1)}), bf16[64,2,4,3584]{3,2,1,0:T(4,128)(2,1)}, u32[]{:S(2)}, u32[]{:S(2)}) async-start(bf16[64,2,4,3584]{3,2,1,0:T(4,128)(2,1)} %bitcast.111), calls=%async_computation | async-start | bytes 7340032 | tf_op jit(solution)/shard_map/all_to_all | solution.py:74
  29.3 26.0 %all_gather.9 = bf16[1,3584,128]{2,1,0:T(8,128)(2,1)} all-gather(bf16[1,448,128]{2,1,0:T(8,128)(2,1)S(1)} %copy-done.6), channel_id=1, replica_groups=mesh['dp'=8,'expert'=64] {'dp'}, dimensions={1}, use_global_device_ids=true | all-gather | bytes 1032192 | tf_op jit(solution)/shard_map/all_gather | solution.py:67
  55.3 24.1 %all_gather.11 = bf16[1,3584,128]{2,1,0:T(8,128)(2,1)} all-gather(bf16[1,448,128]{2,1,0:T(8,128)(2,1)S(1)} %copy-done.7), channel_id=1, replica_groups=mesh['dp'=8,'expert'=64] {'dp'}, dimensions={1}, use_global_device_ids=true | all-gather | bytes 1032192 | tf_op jit(solution)/shard_map/all_gather | solution.py:69
  79.5 24.1 %all_gather.10 = bf16[1,3584,128]{2,1,0:T(8,128)(2,1)} all-gather(bf16[1,448,128]{2,1,0:T(8,128)(2,1)S(1)} %copy-done.8), channel_id=1, replica_groups=mesh['dp'=8,'expert'=64] {'dp'}, dimensions={1}, use_global_device_ids=true | all-gather | bytes 1032192 | tf_op jit(solution)/shard_map/all_gather | solution.py:68
  103.6 10.4 %all-to-all-done = bf16[64,2,4,3584]{3,2,1,0:T(4,128)(2,1)} async-done(((bf16[64,2,4,3584]{3,2,1,0:T(4,128)(2,1)}), bf16[64,2,4,3584]{3,2,1,0:T(4,128)(2,1)}, u32[]{:S(2)}, u32[]{:S(2)}) %all-to-all-start) | async-done | bytes 3670048 | tf_op jit(solution)/shard_map/all_to_all | solution.py:74
  113.9 5.1 %fusion.42 = (bf16[1,64,1,4,3584]{4,3,2,1,0:T(4,128)(2,1)}, bf16[1,64,1,4,3584]{4,3,2,1,0:T(4,128)(2,1)}) fusion(bf16[1,64,2,4,3584]{4,3,2,1,0:T(4,128)(2,1)} %bitcast.12), kind=kLoop, calls=%fused_computation.71 | loop fusion | bytes 7340032 | tf_op jit(solution)/shard_map/slice | solution.py:77
  119.1 2.9 %reshape.115 = bf16[256,3584]{1,0:T(8,128)(2,1)S(1)} reshape(bf16[1,64,1,4,3584]{4,3,2,1,0:T(4,128)(2,1)} %get-tuple-element.21) | data formatting | bytes 3670016 | tf_op jit(solution)/shard_map/reshape.5
  122.0 4.0 %reshape.119 = bf16[256,3584]{1,0:T(8,128)(2,1)} reshape(bf16[1,64,1,4,3584]{4,3,2,1,0:T(4,128)(2,1)} %get-tuple-element.20) | data formatting | bytes 3670016 | tf_op jit(solution)/shard_map/reshape.24
  126.0 2.0 fusion.20
  130.4 0.6 fusion.18
  131.0 1.9 fusion.2
  132.9 4.1 %stack_reshape.9 = bf16[1,64,1,4,3584]{4,3,1,2,0:T(4,128)(2,1)} reshape(bf16[1,256,3584]{2,1,0:T(8,128)(2,1)} %fusion.2) | data formatting | bytes 3670016 | tf_op jit(solution)/shard_map/stack;reshape | solution.py:85
  137.0 3.1 %fusion.1 = bf16[1,256,3584]{2,1,0:T(8,128)(2,1)} fusion(bf16[256,128]{1,0:T(8,128)(2,1)S(1)} %get-tuple-element.25, bf16[1,3584,128]{2,1,0:T(8,128)(2,1)} %all_gather.11), kind=kOutput, calls=%fused_computation.3 | convolution fusion | flops 235798528 | bytes 2818048 | tf_op jit(solution)/shard_map/rh,pfh->prf/dot_general | solution.py:31
  140.1 4.1 %stack_reshape.8 = bf16[1,64,1,4,3584]{4,3,1,2,0:T(4,128)(2,1)} reshape(bf16[1,256,3584]{2,1,0:T(8,128)(2,1)} %fusion.1) | data formatting | bytes 3670016 | tf_op jit(solution)/shard_map/stack;reshape | solution.py:85
  144.1 6.3 %maximum_bitcast_fusion = bf16[64,2,4,3584]{3,2,1,0:T(4,128)(2,1)} fusion(bf16[1,64,1,4,3584]{4,3,2,1,0:T(4,128)(2,1)} %bitcast.112, bf16[1,64,1,4,3584]{4,3,2,1,0:T(4,128)(2,1)} %bitcast.113), kind=kLoop, calls=%fused_computation.21 | loop fusion | flops 1835008 | bytes 7340032 | tf_op jit(solution)/shard_map/convert_element_type | solution.py:93
  150.4 13.0 %all-to-all-start.1 = ((bf16[64,2,4,3584]{3,2,1,0:T(4,128)(2,1)}), bf16[64,2,4,3584]{3,2,1,0:T(4,128)(2,1)}, u32[]{:S(2)}, u32[]{:S(2)}) async-start(bf16[64,2,4,3584]{3,2,1,0:T(4,128)(2,1)} %maximum_bitcast_fusion), calls=%async_computation.1 | async-start | bytes 7340032 | tf_op jit(solution)/shard_map/all_to_all | solution.py:92
  164.6 1.0 copy-done.2
  166.1 1.7 maximum_bitcast_fusion.1
  167.8 4.5 %copy.51 = bf16[3584,384]{1,0:T(8,128)(2,1)} copy(bf16[3584,384]{0,1:T(8,128)(2,1)} %maximum_bitcast_fusion.1) | data formatting | bytes 5505024
  172.3 42.9 %reduce-scatter.4.cloned.1.call-done = bf16[448,384]{1,0:T(8,128)(2,1)} async-done(((bf16[3584,384]{1,0:T(8,128)(2,1)}), bf16[448,384]{1,0:T(8,128)(2,1)}) %reduce-scatter.4.cloned.1.call-update) | async-done | bytes 344080
  215.3 1.1 copy.52
  216.6 0.8 copy.48
  217.4 0.8 copy.49
  218.2 0.8 copy.50
  219.0 29.1 %all-to-all-done.1 = bf16[64,2,4,3584]{3,2,1,0:T(4,128)(2,1)} async-done(((bf16[64,2,4,3584]{3,2,1,0:T(4,128)(2,1)}), bf16[64,2,4,3584]{3,2,1,0:T(4,128)(2,1)}, u32[]{:S(2)}, u32[]{:S(2)}) %all-to-all-start.1) | async-done | bytes 3670048 | tf_op jit(solution)/shard_map/all_to_all | solution.py:92
  248.1 3.6 %bitcast_reduce_fusion = bf16[4,2,4,3584]{3,2,1,0:T(4,128)(2,1)S(1)} fusion(bf16[64,2,4,3584]{3,2,1,0:T(4,128)(2,1)} %all-to-all-done.1), kind=kLoop, calls=%fused_computation.22 | loop fusion | flops 1720320 | bytes 3899392 | tf_op jit(solution)/shard_map/reduce_sum | solution.py:95
  251.9 1.9 fusion.4
  253.8 1.9 fusion.3
  (38 shorter events, 5.3 us)
Async XLA Ops:
  7.2 2.1 copy-start
  14.1 15.1 %copy-start.6 = (bf16[1,448,128]{2,1,0:T(8,128)(2,1)S(1)}, bf16[1,448,128]{2,1,0:T(8,128)(2,1)}, u32[]{:S(2)}) copy-start(bf16[1,448,128]{2,1,0:T(8,128)(2,1)} %param.11) | copy-start | bytes 344068
  14.1 41.2 %copy-start.7 = (bf16[1,448,128]{2,1,0:T(8,128)(2,1)S(1)}, bf16[1,448,128]{2,1,0:T(8,128)(2,1)}, u32[]{:S(2)}) copy-start(bf16[1,448,128]{2,1,0:T(8,128)(2,1)} %param.13) | copy-start | bytes 344068
  14.1 99.8 %all-to-all-start = ((bf16[64,2,4,3584]{3,2,1,0:T(4,128)(2,1)}), bf16[64,2,4,3584]{3,2,1,0:T(4,128)(2,1)}, u32[]{:S(2)}, u32[]{:S(2)}) async-start(bf16[64,2,4,3584]{3,2,1,0:T(4,128)(2,1)} %bitcast.111), calls=%async_computation | async-start | bytes 7340032 | tf_op jit(solution)/shard_map/all_to_all | solution.py:74
  29.3 50.2 %copy-start.8 = (bf16[1,448,128]{2,1,0:T(8,128)(2,1)S(1)}, bf16[1,448,128]{2,1,0:T(8,128)(2,1)}, u32[]{:S(2)}) copy-start(bf16[1,448,128]{2,1,0:T(8,128)(2,1)} %param.12) | copy-start | bytes 344068
  126.0 2.0 copy-start.1
  126.0 2.0 copy-start.3
  128.0 1.2 copy-start.5
  129.2 1.2 copy-start.4
  150.4 97.7 %all-to-all-start.1 = ((bf16[64,2,4,3584]{3,2,1,0:T(4,128)(2,1)}), bf16[64,2,4,3584]{3,2,1,0:T(4,128)(2,1)}, u32[]{:S(2)}, u32[]{:S(2)}) async-start(bf16[64,2,4,3584]{3,2,1,0:T(4,128)(2,1)} %maximum_bitcast_fusion), calls=%async_computation.1 | async-start | bytes 7340032 | tf_op jit(solution)/shard_map/all_to_all | solution.py:92
  163.4 51.8 %reduce-scatter.4.cloned.1.call-start = ((), (), s32[]{:S(2)}) async-start(), calls=%async_computation.3 | async-start | bytes 3096576
  164.2 1.5 copy-start.2
Sparse Core Ops, SparseCore 0:
  172.5 42.7 reduce-scatter.3
where the time goes:
time: 264 us; the launch traced here: 263 us
  waiting for transfers between devices  82.4 us (31%)
  blocking collectives  74.3 us (28%)
  local copies, waits for them, and re-layouts  34 us (13%)
  starting transfers between devices  28.4 us (11%)
  matrix products  15.7 us (6%)
  between operations  14.2 us (5%)
  other arithmetic  13.7 us (5%)
    unnamed x2, waiting for transfers between devices  42.9 us
    all_to_all x1, waiting for transfers between devices, per_device(): lax.all_to_all(results[0].astype(jnp.bfloat16), 'expert', split_axis=0, c...  29.1 us
    all_gather x1, blocking collectives, per_device(): lax.all_gather(w_gate, 'dp', axis=1, tiled=True)  26 us
    all_gather x1, blocking collectives, per_device(): lax.all_gather(w_down, 'dp', axis=1, tiled=True)  24.1 us
    all_gather x1, blocking collectives, per_device(): lax.all_gather(w_up, 'dp', axis=1, tiled=True)  24.1 us
    all_to_all x1, starting transfers between devices, per_device(): lax.all_to_all(outgoing, 'expert', split_axis=0, concat_axis=0, tiled=True)  15.1 us
    all_to_all x1, starting transfers between devices, per_device(): lax.all_to_all(results[0].astype(jnp.bfloat16), 'expert', split_axis=0, c...  13 us
    all_to_all x1, waiting for transfers between devices, per_device(): lax.all_to_all(outgoing, 'expert', split_axis=0, concat_axis=0, tiled=True)  10.4 us
  transfers between devices with their start and end apart: 3, of which 3 were waited for; matrix products, arithmetic and copies ran while one was open for 4% of the time, Pallas kernels for 0%

commit v1 on v0

--- a/solution.py
+++ b/solution.py
@@ -7,6 +7,13 @@
 CAP = 4
 SCALE = 2.0 ** (-16)
 HIGH = lax.Precision.HIGHEST
+
+
+def swapped_in(array, mesh_axis, along):
+    size = lax.axis_size(mesh_axis)
+    blocks = jnp.stack([array for _ in range(size)])
+    blocks = lax.all_to_all(blocks, mesh_axis, split_axis=0, concat_axis=0)
+    return jnp.concatenate(blocks, axis=along)
 
 
 def routing(ids, gates, window, capacity):
@@ -65,7 +72,7 @@
     payload = jnp.stack([slot_tokens, slot_cot], axis=2)
     gate_full, up_full, down_full = (
         lax.all_gather(w_gate, "dp", axis=1, tiled=True),
-        lax.all_gather(w_up, "dp", axis=1, tiled=True),
+        swapped_in(w_up, "dp", 1),
         lax.all_gather(w_down, "dp", axis=1, tiled=True),
     )
     outgoing = jnp.broadcast_to(payload, (window, SPLIT, 2, CAP, width)).reshape(

time: 264 us -> 278 us (1.053)
  waiting for transfers between devices: 82.4 us -> 118 us
  blocking collectives: 74.3 us -> 50.2 us
    all_to_all x1, waiting for transfers between devices: 10.4 us -> 34.5 us  [per_device(): lax.all_to_all(outgoing, 'expert', split_axis=0, concat_axis=0, tiled=True)]
    all_gather x1 -> x0, blocking collectives: 24.1 us -> none  [per_device(): lax.all_gather(w_up, 'dp', axis=1, tiled=True)]
    all_to_all x0 -> x1, waiting for transfers between devices: none -> 11.8 us  [swapped_in(): blocks = lax.all_to_all(blocks, mesh_axis, split_axis=0, concat_axis=0)]
    all_to_all x0 -> x1, starting transfers between devices: none -> 6.82 us  [swapped_in(): blocks = lax.all_to_all(blocks, mesh_axis, split_axis=0, concat_axis=0)]
    all_to_all x1, starting transfers between devices: 13 us -> 6.26 us  [per_device(): lax.all_to_all(results[0].astype(jnp.bfloat16), 'expert', split_axis=0, c...]
    all_to_all x1, waiting for transfers between devices: 29.1 us -> 32.6 us  [per_device(): lax.all_to_all(results[0].astype(jnp.bfloat16), 'expert', split_axis=0, c...]
    unnamed x2, waiting for transfers between devices: 42.9 us -> 39.4 us
    unnamed x23 -> x21, local copies, waits for them, and re-layouts: 10.3 us -> 9.2 us
  transfers between devices with their start and end apart: 3 -> 4, of which waited for: 3 -> 4; matrix products, arithmetic and copies ran while one was open for 4% -> 9% of each run, Pallas kernels for 0% -> 0%
where the time goes in v1:
time: 278 us; the launch traced here: 277 us
  waiting for transfers between devices  118 us (42%)
  blocking collectives  50.2 us (18%)
  local copies, waits for them, and re-layouts  33.9 us (12%)
  starting transfers between devices  28.5 us (10%)
  matrix products  18.1 us (7%)
  between operations  14.2 us (5%)
  other arithmetic  13.7 us (5%)
    unnamed x2, waiting for transfers between devices  39.4 us
    all_to_all x1, waiting for transfers between devices, per_device(): lax.all_to_all(outgoing, 'expert', split_axis=0, concat_axis=0, tiled=True)  34.5 us
    all_to_all x1, waiting for transfers between devices, per_device(): lax.all_to_all(results[0].astype(jnp.bfloat16), 'expert', split_axis=0, c...  32.6 us
    all_gather x1, blocking collectives, per_device(): lax.all_gather(w_gate, 'dp', axis=1, tiled=True)  26 us
    all_gather x1, blocking collectives, per_device(): lax.all_gather(w_down, 'dp', axis=1, tiled=True)  24.1 us
    all_to_all x1, starting transfers between devices, per_device(): lax.all_to_all(outgoing, 'expert', split_axis=0, concat_axis=0, tiled=True)  15.1 us
    all_to_all x1, waiting for transfers between devices, swapped_in(): blocks = lax.all_to_all(blocks, mesh_axis, split_axis=0, concat_axis=0)  11.8 us
    unnamed x21, local copies, waits for them, and re-layouts  9.2 us
  transfers between devices with their start and end apart: 4, of which 4 were waited for; matrix products, arithmetic and copies ran while one was open for 9% of the time, Pallas kernels for 0%

profile of v1, /device:TPU:1, one launch (start us, length us, event | category | flops | bytes accessed | tf_op | source)
XLA Modules:
  0.0 276.8 jit_solution(656379216648197908)
XLA Ops:
  9.5 1.4 fusion.11
  11.2 2.9 %broadcast_in_dim.54 = bf16[4,16,2,4,3584]{4,3,2,1,0:T(4,128)(2,1)} broadcast(bf16[4,2,4,3584]{3,2,1,0:T(4,128)(2,1)S(1)} %copy.43), dimensions={0,2,3,4} | broadcast | bytes 3899392 | tf_op jit(solution)/shard_map/broadcast_in_dim | solution.py:78
  14.1 15.1 %all-to-all-start = ((bf16[64,2,4,3584]{3,2,1,0:T(4,128)(2,1)}), bf16[64,2,4,3584]{3,2,1,0:T(4,128)(2,1)}, u32[]{:S(2)}, u32[]{:S(2)}) async-start(bf16[64,2,4,3584]{3,2,1,0:T(4,128)(2,1)} %bitcast.108), calls=%async_computation | async-start | bytes 7340032 | tf_op jit(solution)/shard_map/all_to_all | solution.py:81
  29.3 26.0 %all_gather.6 = bf16[1,3584,128]{2,1,0:T(8,128)(2,1)} all-gather(bf16[1,448,128]{2,1,0:T(8,128)(2,1)S(1)} %copy-done.5), channel_id=1, replica_groups=mesh['dp'=8,'expert'=64] {'dp'}, dimensions={1}, use_global_device_ids=true | all-gather | bytes 1032192 | tf_op jit(solution)/shard_map/all_gather | solution.py:74
  55.3 24.1 %all_gather.7 = bf16[1,3584,128]{2,1,0:T(8,128)(2,1)} all-gather(bf16[1,448,128]{2,1,0:T(8,128)(2,1)S(1)} %copy-done.6), channel_id=1, replica_groups=mesh['dp'=8,'expert'=64] {'dp'}, dimensions={1}, use_global_device_ids=true | all-gather | bytes 1032192 | tf_op jit(solution)/shard_map/all_gather | solution.py:76
  79.4 34.5 %all-to-all-done = bf16[64,2,4,3584]{3,2,1,0:T(4,128)(2,1)} async-done(((bf16[64,2,4,3584]{3,2,1,0:T(4,128)(2,1)}), bf16[64,2,4,3584]{3,2,1,0:T(4,128)(2,1)}, u32[]{:S(2)}, u32[]{:S(2)}) %all-to-all-start) | async-done | bytes 3670048 | tf_op jit(solution)/shard_map/all_to_all | solution.py:81
  113.9 1.0 stack.27
  115.0 6.8 %all-to-all-start.1 = ((bf16[8,1,448,128]{3,2,1,0:T(8,128)(2,1)}), bf16[8,1,448,128]{3,2,1,0:T(8,128)(2,1)}, u32[]{:S(2)}, u32[]{:S(2)}) async-start(bf16[8,1,448,128]{3,2,1,0:T(8,128)(2,1)} %stack.27), calls=%async_computation.1 | async-start | bytes 1835008 | tf_op jit(solution)/shard_map/all_to_all | solution.py:15
  121.8 5.1 %fusion.39 = (bf16[1,64,1,4,3584]{4,3,2,1,0:T(4,128)(2,1)}, bf16[1,64,1,4,3584]{4,3,2,1,0:T(4,128)(2,1)}) fusion(bf16[1,64,2,4,3584]{4,3,2,1,0:T(4,128)(2,1)} %bitcast.12), kind=kLoop, calls=%fused_computation.68 | loop fusion | bytes 7340032 | tf_op jit(solution)/shard_map/slice | solution.py:84
  126.9 2.9 %reshape.121 = bf16[256,3584]{1,0:T(8,128)(2,1)S(1)} reshape(bf16[1,64,1,4,3584]{4,3,2,1,0:T(4,128)(2,1)} %get-tuple-element.21) | data formatting | bytes 3670016 | tf_op jit(solution)/shard_map/reshape.5
  129.9 4.0 %reshape.125 = bf16[256,3584]{1,0:T(8,128)(2,1)} reshape(bf16[1,64,1,4,3584]{4,3,2,1,0:T(4,128)(2,1)} %get-tuple-element.20) | data formatting | bytes 3670016 | tf_op jit(solution)/shard_map/reshape.26
  133.9 1.9 fusion.17
  136.5 11.8 %all-to-all-done.1 = bf16[8,1,448,128]{3,2,1,0:T(8,128)(2,1)} async-done(((bf16[8,1,448,128]{3,2,1,0:T(8,128)(2,1)}), bf16[8,1,448,128]{3,2,1,0:T(8,128)(2,1)}, u32[]{:S(2)}, u32[]{:S(2)}) %all-to-all-start.1) | async-done | bytes 917536 | tf_op jit(solution)/shard_map/all_to_all | solution.py:15
  148.3 1.9 multiply_convert_fusion.2
  150.8 3.1 %fusion.2 = bf16[1,256,3584]{2,1,0:T(8,128)(2,1)} fusion(f32[256,3584]{1,0:T(8,128)S(1)} %fusion.15, bf16[256,128]{1,0:T(8,128)(2,1)S(1)} %get-tuple-element.27, bf16[3584,128]{1,0:T(8,128)(2,1)} %bitcast.15), kind=kOutput, calls=%fused_computation.4 | convolution fusion | flops 236716032 | bytes 6488064 | tf_op jit(solution)/shard_map/rh,pfh->prf/dot_general | solution.py:44
  153.9 4.1 %stack_reshape.9 = bf16[1,64,1,4,3584]{4,3,1,2,0:T(4,128)(2,1)} reshape(bf16[1,256,3584]{2,1,0:T(8,128)(2,1)} %fusion.2) | data formatting | bytes 3670016 | tf_op jit(solution)/shard_map/stack;reshape | solution.py:92
  158.0 3.1 %fusion.1 = bf16[1,256,3584]{2,1,0:T(8,128)(2,1)} fusion(bf16[256,128]{1,0:T(8,128)(2,1)S(1)} %get-tuple-element.25, bf16[1,3584,128]{2,1,0:T(8,128)(2,1)} %all_gather.7), kind=kOutput, calls=%fused_computation.3 | convolution fusion | flops 235798528 | bytes 2818048 | tf_op jit(solution)/shard_map/rh,pfh->prf/dot_general | solution.py:38
  161.1 4.1 %stack_reshape.8 = bf16[1,64,1,4,3584]{4,3,1,2,0:T(4,128)(2,1)} reshape(bf16[1,256,3584]{2,1,0:T(8,128)(2,1)} %fusion.1) | data formatting | bytes 3670016 | tf_op jit(solution)/shard_map/stack;reshape | solution.py:92
  165.2 6.3 %maximum_bitcast_fusion = bf16[64,2,4,3584]{3,2,1,0:T(4,128)(2,1)} fusion(bf16[1,64,1,4,3584]{4,3,2,1,0:T(4,128)(2,1)} %bitcast.109, bf16[1,64,1,4,3584]{4,3,2,1,0:T(4,128)(2,1)} %bitcast.110), kind=kLoop, calls=%fused_computation.21 | loop fusion | flops 1835008 | bytes 7340032 | tf_op jit(solution)/shard_map/convert_element_type | solution.py:100
  171.4 6.3 %all-to-all-start.2 = ((bf16[64,2,4,3584]{3,2,1,0:T(4,128)(2,1)}), bf16[64,2,4,3584]{3,2,1,0:T(4,128)(2,1)}, u32[]{:S(2)}, u32[]{:S(2)}) async-start(bf16[64,2,4,3584]{3,2,1,0:T(4,128)(2,1)} %maximum_bitcast_fusion), calls=%async_computation.2 | async-start | bytes 7340032 | tf_op jit(solution)/shard_map/all_to_all | solution.py:99
  178.9 1.0 copy-done.2
  180.4 1.7 maximum_bitcast_fusion.1
  182.1 4.5 %copy.51 = bf16[3584,384]{1,0:T(8,128)(2,1)} copy(bf16[3584,384]{0,1:T(8,128)(2,1)} %maximum_bitcast_fusion.1) | data formatting | bytes 5505024
  186.6 39.4 %reduce-scatter.4.cloned.1.call-done = bf16[448,384]{1,0:T(8,128)(2,1)} async-done(((bf16[3584,384]{1,0:T(8,128)(2,1)}), bf16[448,384]{1,0:T(8,128)(2,1)}) %reduce-scatter.4.cloned.1.call-update) | async-done | bytes 344080
  226.0 1.1 copy.52
  227.3 0.8 copy.48
  228.1 0.8 copy.49
  228.9 0.8 copy.50
  229.8 32.6 %all-to-all-done.2 = bf16[64,2,4,3584]{3,2,1,0:T(4,128)(2,1)} async-done(((bf16[64,2,4,3584]{3,2,1,0:T(4,128)(2,1)}), bf16[64,2,4,3584]{3,2,1,0:T(4,128)(2,1)}, u32[]{:S(2)}, u32[]{:S(2)}) %all-to-all-start.2) | async-done | bytes 3670048 | tf_op jit(solution)/shard_map/all_to_all | solution.py:99
  262.4 3.6 %bitcast_reduce_fusion = bf16[4,2,4,3584]{3,2,1,0:T(4,128)(2,1)S(1)} fusion(bf16[64,2,4,3584]{3,2,1,0:T(4,128)(2,1)} %all-to-all-done.2), kind=kLoop, calls=%fused_computation.22 | loop fusion | flops 1720320 | bytes 3899392 | tf_op jit(solution)/shard_map/reduce_sum | solution.py:102
  266.2 1.9 fusion.4
  268.0 1.9 fusion.3
  (38 shorter events, 5.8 us)
Async XLA Ops:
  7.2 2.1 copy-start
  14.1 15.1 %copy-start.5 = (bf16[1,448,128]{2,1,0:T(8,128)(2,1)S(1)}, bf16[1,448,128]{2,1,0:T(8,128)(2,1)}, u32[]{:S(2)}) copy-start(bf16[1,448,128]{2,1,0:T(8,128)(2,1)} %param.11) | copy-start | bytes 344068
  14.1 41.2 %copy-start.6 = (bf16[1,448,128]{2,1,0:T(8,128)(2,1)S(1)}, bf16[1,448,128]{2,1,0:T(8,128)(2,1)}, u32[]{:S(2)}) copy-start(bf16[1,448,128]{2,1,0:T(8,128)(2,1)} %param.13) | copy-start | bytes 344068
  14.1 99.8 %all-to-all-start = ((bf16[64,2,4,3584]{3,2,1,0:T(4,128)(2,1)}), bf16[64,2,4,3584]{3,2,1,0:T(4,128)(2,1)}, u32[]{:S(2)}, u32[]{:S(2)}) async-start(bf16[64,2,4,3584]{3,2,1,0:T(4,128)(2,1)} %bitcast.108), calls=%async_computation | async-start | bytes 7340032 | tf_op jit(solution)/shard_map/all_to_all | solution.py:81
  29.3 84.7 %copy-start.7 = (bf16[1,448,128]{2,1,0:T(8,128)(2,1)S(1)}, bf16[1,448,128]{2,1,0:T(8,128)(2,1)}, u32[]{:S(2)}) copy-start(bf16[1,448,128]{2,1,0:T(8,128)(2,1)} %param.12) | copy-start | bytes 344068
  115.0 33.3 %all-to-all-start.1 = ((bf16[8,1,448,128]{3,2,1,0:T(8,128)(2,1)}), bf16[8,1,448,128]{3,2,1,0:T(8,128)(2,1)}, u32[]{:S(2)}, u32[]{:S(2)}) async-start(bf16[8,1,448,128]{3,2,1,0:T(8,128)(2,1)} %stack.27), calls=%async_computation.1 | async-start | bytes 1835008 | tf_op jit(solution)/shard_map/all_to_all | solution.py:15
  133.9 2.0 copy-start.1
  133.9 2.0 copy-start.3
  148.3 1.9 copy-start.4
  171.4 90.9 %all-to-all-start.2 = ((bf16[64,2,4,3584]{3,2,1,0:T(4,128)(2,1)}), bf16[64,2,4,3584]{3,2,1,0:T(4,128)(2,1)}, u32[]{:S(2)}, u32[]{:S(2)}) async-start(bf16[64,2,4,3584]{3,2,1,0:T(4,128)(2,1)} %maximum_bitcast_fusion), calls=%async_computation.2 | async-start | bytes 7340032 | tf_op jit(solution)/shard_map/all_to_all | solution.py:99
  177.7 48.3 %reduce-scatter.4.cloned.1.call-start = ((), (), s32[]{:S(2)}) async-start(), calls=%async_computation.4 | async-start | bytes 3096576
  178.4 1.5 copy-start.2
Sparse Core Ops, SparseCore 0:
  186.7 39.2 reduce-scatter.3
